TPU v7x, 32 devices: a whole 2x2x4 slice. The times are simulated.
32 devices in a mesh: groups: 2 (over y), expert: 4 (over z), tensor: 4 (over x, core).
Axes of the slice: x: 2, y: 2, z: 4, core: 2. Of those that a mesh axis runs over, the one named last changes fastest.
Arguments:
- tokens: bfloat16 [1024, 2560], P(('groups', 'expert'), 'tensor'), parts along dimension 0, may hold values from -6 to 6
- route_scale: float32 [1024], P(('groups', 'expert')), parts along dimension 0, may hold values from 0.25 to 1
- expert_ids: int32 [1024, 1], P(('groups', 'expert')), parts along dimension 0, may hold values from 0 to 1; in each aligned block of 128 rows (0 to 127, 128 to 255, ...) at most 128 rows name the same one
- gate_weight: bfloat16 [4, 2560, 2048], P('expert', None, 'tensor'), may hold values from -0.125 to 0.125
- up_weight: bfloat16 [4, 2560, 2048], P('expert', None, 'tensor'), may hold values from -0.125 to 0.125
- down_weight: bfloat16 [4, 2048, 2560], P('expert', 'tensor'), may hold values from -0.09375 to 0.09375
Outputs:
- mixed: bfloat16 [1024, 2560], P(('groups', 'expert'), 'tensor'), parts along dimension 0
There are 2 independent parts, one for each index of `groups`. A program takes and returns all parts, laid end to end along the dimension named above; an argument that names none is the same for every part. Nothing has to cross between parts.
Inputs may be any that keep to these rules, and one draw needn't show every extreme that they name: `expert_ids`: within the rows of one index of the expert axis (aligned blocks of 128 tokens) no expert is named by more than 128 tokens, and in some block one expert is named by exactly 128 tokens.
All inputs are finite; a program needn't handle non-finite values.
Results may differ from a plain program's by a relative error of at most 0.019.
Values may be sent and summed in bfloat16 or wider, within the bound.
No kernel may reach another device: no remote copies, remote signals or barrier semaphores. Data moves between devices by JAX's collectives and lax.ppermute only.
A program may use at most 64 MiB of HBM per device.

v0:
```python
import jax
import jax.numpy as jnp
from jax import lax
from jax.sharding import PartitionSpec as P

SPAN = 2


def local(tokens, route_scale, expert_ids, gate_weight, up_weight, down_weight):
    tok_rows = tokens.shape[0]
    n_devices = lax.axis_size("expert")
    experts = n_devices // SPAN
    capacity = min(tok_rows, 2 * tok_rows * SPAN // n_devices)
    routed = expert_ids[:, 0]
    one_hot = (routed[:, None] == jnp.arange(experts, dtype=jnp.int32)[None, :]).astype(jnp.int32)
    slot_rank = jnp.sum((jnp.cumsum(one_hot, axis=0) - one_hot) * one_hot, axis=1)
    flat_slot = routed * capacity + slot_rank
    placing = (
        flat_slot[None, :] == jnp.arange(experts * capacity, dtype=jnp.int32)[:, None]
    ).astype(jnp.bfloat16)
    scaled = (tokens.astype(jnp.float32) * route_scale[:, None]).astype(jnp.bfloat16)
    gate_local = gate_weight[0]
    up_local = up_weight[0]
    down_local = down_weight[0]
    full_rows = lax.all_gather(scaled, "tensor", axis=1, tiled=True)
    width = full_rows.shape[1]
    packed = jnp.dot(placing, full_rows, preferred_element_type=jnp.float32).astype(jnp.bfloat16)
    outgoing = jnp.repeat(packed.reshape(experts, capacity, width), SPAN, axis=0)
    arrived = lax.all_to_all(outgoing, "expert", split_axis=0, concat_axis=0, tiled=True)
    slot_rows = arrived.reshape(n_devices * capacity, width)
    gate_act = jnp.dot(slot_rows, gate_local, preferred_element_type=jnp.float32)
    up_act = jnp.dot(slot_rows, up_local, preferred_element_type=jnp.float32)
    hidden = (jax.nn.silu(gate_act) * up_act).astype(jnp.bfloat16)
    partial_value = jnp.dot(hidden, down_local, preferred_element_type=jnp.float32)
    width = partial_value.shape[1]
    outgoing_back = partial_value.astype(jnp.bfloat16).reshape(n_devices, capacity, width)
    returned = lax.all_to_all(outgoing_back, "expert", split_axis=0, concat_axis=0, tiled=True)
    paired = jnp.sum(returned.astype(jnp.float32).reshape(experts, SPAN, capacity, width), axis=1)
    picked = jnp.take(paired.reshape(experts * capacity, width), flat_slot, axis=0)
    summed = lax.psum_scatter(
        picked.astype(jnp.bfloat16), "tensor", scatter_dimension=1, tiled=True
    )
    return summed


def solution(mesh):
    placed = (
        P(("groups", "expert"), "tensor"),
        P(("groups", "expert")),
        P(("groups", "expert"), None),
        P("expert", None, "tensor"),
        P("expert", None, "tensor"),
        P("expert", "tensor", None),
    )
    return jax.shard_map(
        local,
        mesh=mesh,
        in_specs=placed,
        out_specs=P(("groups", "expert"), "tensor"),
        check_vma=False,
    )
```

profile of v0, /device:TPU:0, one launch (start us, length us, event | category | flops | bytes accessed | tf_op | source)
XLA Modules:
  0.0 200.1 jit_solution(4771933198922784884)
XLA Ops:
  6.5 0.0 copy-start
  6.5 0.9 fusion.15
  7.4 0.2 reduce_window_sum.11
  7.6 0.8 select_reduce_fusion
  8.4 0.7 multiply_add_fusion
  9.1 1.0 multiply_convert_fusion
  10.1 9.3 %all_gather.3 = bf16[128,2560]{1,0:T(8,128)(2,1)S(1)} all-gather(bf16[128,640]{1,0:T(8,128)(2,1)S(1)} %multiply_convert_fusion), channel_id=1, replica_groups=mesh['groups'=2,'expert'=4,'tensor'=4] {'tensor'}, dimensions={1}, use_global_device_ids=true | all-gather | bytes 819200 | tf_op jit(solution)/shard_map/all_gather | solution.py:25
  19.4 0.5 convolution_convert_fusion.1
  19.9 0.2 broadcast_in_dim.18
  20.2 0.0 copy-start.3
  20.2 64.9 %all_to_all.10 = bf16[4,128,2560]{2,1,0:T(8,128)(2,1)S(1)} all-to-all(bf16[4,128,2560]{2,1,0:T(8,128)(2,1)S(1)} %bitcast.39), channel_id=1, replica_groups=mesh['groups'=2,'expert'=4,'tensor'=4] {'expert'}, dimensions={0} | all-to-all | bytes 5242880 | tf_op jit(solution)/shard_map/all_to_all | solution.py:29
  85.1 1.5 copy-done.1
  86.6 2.5 %fusion.3 = f32[512,512]{1,0:T(8,128)} fusion(bf16[512,2560]{1,0:T(8,128)(2,1)S(1)} %bitcast.42, bf16[1,2560,512]{2,1,0:T(8,128)(2,1)S(1)} %copy-done.3), kind=kOutput, calls=%fused_computation.7 | convolution fusion | flops 1342177280 | bytes 6291456 | tf_op jit(solution)/shard_map/dot_general | solution.py:31
  89.1 7.2 %convolution_convert_fusion = bf16[512,2560]{1,0:T(8,128)(2,1)} fusion(bf16[1,512,2560]{2,1,0:T(8,128)(2,1)S(1)} %copy-done, bf16[512,2560]{1,0:T(8,128)(2,1)} %bitcast.43, bf16[1,2560,512]{2,1,0:T(8,128)(2,1)} %param.10, f32[512,512]{1,0:T(8,128)} %fusion.3), kind=kOutput, calls=%fused_computation.2 | convolution fusion | flops 2687238144 | bytes 11534336 | tf_op jit(solution)/shard_map/dot_general | solution.py:34
  96.4 4.7 %all-to-all-start.1 = ((bf16[4,128,2560]{2,1,0:T(8,128)(2,1)}), bf16[4,128,2560]{2,1,0:T(8,128)(2,1)}, u32[]{:S(2)}, u32[]{:S(2)}) async-start(bf16[4,128,2560]{2,1,0:T(8,128)(2,1)} %bitcast.41), calls=%async_computation.1 | async-start | bytes 5242880 | tf_op jit(solution)/shard_map/all_to_all | solution.py:37
  101.1 0.0 reduce-scatter.4.cloned.1.call-start
  101.1 59.1 %all-to-all-done.1 = bf16[4,128,2560]{2,1,0:T(8,128)(2,1)} async-done(((bf16[4,128,2560]{2,1,0:T(8,128)(2,1)}), bf16[4,128,2560]{2,1,0:T(8,128)(2,1)}, u32[]{:S(2)}, u32[]{:S(2)}) %all-to-all-start.1) | async-done | bytes 2621472 | tf_op jit(solution)/shard_map/all_to_all | solution.py:37
  160.2 3.6 %convert_reduce_fusion = bf16[2,128,2560]{2,1,0:T(8,128)(2,1)} fusion(bf16[4,128,2560]{2,1,0:T(8,128)(2,1)} %all-to-all-done.1), kind=kLoop, calls=%fused_computation.1 | loop fusion | flops 1966080 | bytes 3932160 | tf_op jit(solution)/shard_map/reduce_sum | solution.py:38
  163.8 3.1 %gather_fusion = bf16[128,2560]{1,0:T(8,128)(2,1)S(1)} fusion(bf16[256,2560]{1,0:T(8,128)(2,1)} %bitcast.38, s32[1024]{0:T(1024)S(1)} %pad_clamp_fusion), kind=kCustom, calls=%fused_computation | custom fusion | bytes 1311232 | tf_op jit(solution)/shard_map/jit(_take)/gather | solution.py:39
  167.0 1.0 select_convert_fusion
  168.0 2.2 %copy.7 = bf16[128,2560]{0,1:T(8,128)(2,1)} copy(bf16[128,2560]{1,0:T(8,128)(2,1)} %select_convert_fusion) | data formatting | bytes 1310720
  170.2 0.0 reduce-scatter.4.cloned.1.call-update
  170.2 21.3 %reduce-scatter.4.cloned.1.call-done = bf16[640,128]{1,0:T(8,128)(2,1)} async-done(((bf16[2560,128]{1,0:T(8,128)(2,1)}), bf16[640,128]{1,0:T(8,128)(2,1)}) %reduce-scatter.4.cloned.1.call-update) | async-done | bytes 163856
  191.5 1.7 copy.8
  (7 shorter events, 0.0 us)
Async XLA Ops:
  6.5 82.6 %copy-start = (bf16[1,512,2560]{2,1,0:T(8,128)(2,1)S(1)}, bf16[1,512,2560]{2,1,0:T(8,128)(2,1)}, u32[]{:S(2)}) copy-start(bf16[1,512,2560]{2,1,0:T(8,128)(2,1)} %param.11) | copy-start | bytes 7864324
  20.2 66.4 %copy-start.3 = (bf16[1,2560,512]{2,1,0:T(8,128)(2,1)S(1)}, bf16[1,2560,512]{2,1,0:T(8,128)(2,1)}, u32[]{:S(2)}) copy-start(bf16[1,2560,512]{2,1,0:T(8,128)(2,1)} %param.9) | copy-start | bytes 7864324
  85.1 1.5 copy-start.1
  96.4 4.7 %copy-start.2 = (s32[128,1]{0,1:T(1,128)S(1)}, s32[128,1]{0,1:T(1,128)}, u32[]{:S(2)}) copy-start(s32[128,1]{0,1:T(1,128)} %param.8) | copy-start | bytes 1540
  96.4 63.9 %all-to-all-start.1 = ((bf16[4,128,2560]{2,1,0:T(8,128)(2,1)}), bf16[4,128,2560]{2,1,0:T(8,128)(2,1)}, u32[]{:S(2)}, u32[]{:S(2)}) async-start(bf16[4,128,2560]{2,1,0:T(8,128)(2,1)} %bitcast.41), calls=%async_computation.1 | async-start | bytes 5242880 | tf_op jit(solution)/shard_map/all_to_all | solution.py:37
  101.1 90.5 %reduce-scatter.4.cloned.1.call-start = ((), (), s32[]{:S(2)}) async-start(), calls=%async_computation.3 | async-start | bytes 819200
Sparse Core Ops, SparseCore 0:
  170.3 21.1 reduce-scatter.3
where the time goes:
time: 201 us; the launch traced here: 200 us
  waiting for transfers between devices  80.4 us (40%)
  blocking collectives  74.2 us (37%)
  between operations  13.5 us (7%)
  matrix products  10.3 us (5%)
  local copies, waits for them, and re-layouts  8.75 us (4%)
  other arithmetic  8.23 us (4%)
  starting transfers between devices  4.72 us (2%)
    all_to_all x1, blocking collectives, local(): lax.all_to_all(outgoing, 'expert', split_axis=0, concat_axis=0, tiled=True)  64.9 us
    all_to_all x1, waiting for transfers between devices, local(): lax.all_to_all(outgoing_back, 'expert', split_axis=0, concat_axis=0, tile...  59.1 us
    unnamed x2, waiting for transfers between devices  21.4 us
    all_gather x1, blocking collectives, local(): full_rows = lax.all_gather(scaled, 'tensor', axis=1, tiled=True)  9.33 us
    dot_general x1, matrix products, local(): jnp.dot(hidden, down_local, preferred_element_type=jnp.float32)  7.24 us
    unnamed x10, local copies, waits for them, and re-layouts  5.42 us
    all_to_all x1, starting transfers between devices, local(): lax.all_to_all(outgoing_back, 'expert', split_axis=0, concat_axis=0, tile...  4.68 us
  transfers between devices with their start and end apart: 2, of which 2 were waited for; matrix products, arithmetic and copies ran while one was open for 0% of the time, Pallas kernels for 0%

commit v1 on v0

--- a/solution.py
+++ b/solution.py
@@ -22,7 +22,14 @@
     gate_local = gate_weight[0]
     up_local = up_weight[0]
     down_local = down_weight[0]
-    full_rows = lax.all_gather(scaled, "tensor", axis=1, tiled=True)
+    ring = [scaled]
+    for hop in range(3):
+        ring.append(lax.ppermute(ring[-1], "tensor", [(dev, (dev + 1) % 4) for dev in range(4)]))
+    full_rows = jnp.roll(
+        jnp.concatenate(ring[::-1], axis=1),
+        (lax.axis_index("tensor") + 1) * ring[0].shape[1],
+        axis=1,
+    )
     width = full_rows.shape[1]
     packed = jnp.dot(placing, full_rows, preferred_element_type=jnp.float32).astype(jnp.bfloat16)
     outgoing = jnp.repeat(packed.reshape(experts, capacity, width), SPAN, axis=0)

time: 201 us -> 203 us (level)
  waiting for transfers between devices: 80.4 us -> 91.3 us
  blocking collectives: 74.2 us -> 64.5 us
    ppermute x0 -> x3, waiting for transfers between devices: none -> 12 us  [local(): lax.ppermute(ring[-1], 'tensor', [(dev, (dev + 1) % 4) for dev in range(4)])]
    all_gather x1 -> x0, blocking collectives: 9.33 us -> none  [local(): full_rows = lax.all_gather(scaled, 'tensor', axis=1, tiled=True)]
    unnamed x10 -> x20, local copies, waits for them, and re-layouts: 5.42 us -> 5.54 us
  transfers between devices with their start and end apart: 2 -> 5, of which waited for: 2 -> 5; matrix products, arithmetic and copies ran while one was open for 0% -> 1% of each run, Pallas kernels for 0% -> 0%
where the time goes in v1:
time: 203 us; the launch traced here: 202 us
  waiting for transfers between devices  91.3 us (45%)
  blocking collectives  64.5 us (32%)
  between operations  13.6 us (7%)
  matrix products  10.4 us (5%)
  local copies, waits for them, and re-layouts  8.87 us (4%)
  other arithmetic  8.4 us (4%)
  starting transfers between devices  5.23 us (3%)
    all_to_all x1, blocking collectives, local(): lax.all_to_all(outgoing, 'expert', split_axis=0, concat_axis=0, tiled=True)  64.5 us
    all_to_all x1, waiting for transfers between devices, local(): lax.all_to_all(outgoing_back, 'expert', split_axis=0, concat_axis=0, tile...  58.5 us
    unnamed x2, waiting for transfers between devices  20.8 us
    ppermute x3, waiting for transfers between devices, local(): lax.ppermute(ring[-1], 'tensor', [(dev, (dev + 1) % 4) for dev in range(4)])  12 us
    dot_general x1, matrix products, local(): jnp.dot(hidden, down_local, preferred_element_type=jnp.float32)  7.24 us
    unnamed x20, local copies, waits for them, and re-layouts  5.54 us
    all_to_all x1, starting transfers between devices, local(): lax.all_to_all(outgoing_back, 'expert', split_axis=0, concat_axis=0, tile...  4.68 us
  transfers between devices with their start and end apart: 5, of which 5 were waited for; matrix products, arithmetic and copies ran while one was open for 1% of the time, Pallas kernels for 0%

profile of v1, /device:TPU:0, one launch (start us, length us, event | category | flops | bytes accessed | tf_op | source)
XLA Modules:
  0.0 202.2 jit_solution(2377844881843248434)
XLA Ops:
  6.5 1.2 multiply_convert_fusion
  7.7 0.5 collective-permute-start
  8.2 4.9 %collective-permute-done = bf16[128,640]{1,0:T(8,128)(2,1)S(1)} collective-permute-done((bf16[128,640]{1,0:T(8,128)(2,1)S(1)}, bf16[128,640]{1,0:T(8,128)(2,1)S(1)}, u32[]{:S(2)}, u32[]{:S(2)}) %collective-permute-start) | collective-permute-done | bytes 163872 | tf_op jit(solution)/shard_map/ppermute | solution.py:27
  13.1 0.7 fusion.16
  13.9 0.2 reduce_window_sum.11
  14.1 0.8 select_reduce_fusion
  14.9 3.0 %collective-permute-done.1 = bf16[128,640]{1,0:T(8,128)(2,1)S(1)} collective-permute-done((bf16[128,640]{1,0:T(8,128)(2,1)S(1)}, bf16[128,640]{1,0:T(8,128)(2,1)S(1)}, u32[]{:S(2)}, u32[]{:S(2)}) %collective-permute-start.1) | collective-permute-done | bytes 163872 | tf_op jit(solution)/shard_map/ppermute | solution.py:27
  17.9 0.7 multiply_add_fusion
  18.5 4.1 %collective-permute-done.2 = bf16[128,640]{1,0:T(8,128)(2,1)S(1)} collective-permute-done((bf16[128,640]{1,0:T(8,128)(2,1)S(1)}, bf16[128,640]{1,0:T(8,128)(2,1)S(1)}, u32[]{:S(2)}, u32[]{:S(2)}) %collective-permute-start.2) | collective-permute-done | bytes 163872 | tf_op jit(solution)/shard_map/ppermute | solution.py:27
  22.9 0.1 constant_dynamic-update-slice_fusion
  23.0 0.6 convolution_convert_fusion.1
  23.6 0.2 broadcast_in_dim.18
  23.9 64.5 %all_to_all.10 = bf16[4,128,2560]{2,1,0:T(8,128)(2,1)S(1)} all-to-all(bf16[4,128,2560]{2,1,0:T(8,128)(2,1)S(1)} %bitcast.38), channel_id=1, replica_groups=mesh['groups'=2,'expert'=4,'tensor'=4] {'expert'}, dimensions={0} | all-to-all | bytes 5242880 | tf_op jit(solution)/shard_map/all_to_all | solution.py:36
  88.4 1.5 copy-done.1
  89.9 2.5 %fusion.3 = f32[512,512]{1,0:T(8,128)} fusion(bf16[512,2560]{1,0:T(8,128)(2,1)S(1)} %bitcast.41, bf16[1,2560,512]{2,1,0:T(8,128)(2,1)S(1)} %copy-done.5), kind=kOutput, calls=%fused_computation.7 | convolution fusion | flops 1342177280 | bytes 6291456 | tf_op jit(solution)/shard_map/dot_general | solution.py:38
  92.4 7.2 %convolution_convert_fusion = bf16[512,2560]{1,0:T(8,128)(2,1)} fusion(bf16[1,512,2560]{2,1,0:T(8,128)(2,1)S(1)} %copy-done, bf16[512,2560]{1,0:T(8,128)(2,1)} %bitcast.42, bf16[1,2560,512]{2,1,0:T(8,128)(2,1)} %param.10, f32[512,512]{1,0:T(8,128)} %fusion.3), kind=kOutput, calls=%fused_computation.2 | convolution fusion | flops 2687238144 | bytes 11534336 | tf_op jit(solution)/shard_map/dot_general | solution.py:41
  99.6 4.7 %all-to-all-start.1 = ((bf16[4,128,2560]{2,1,0:T(8,128)(2,1)}), bf16[4,128,2560]{2,1,0:T(8,128)(2,1)}, u32[]{:S(2)}, u32[]{:S(2)}) async-start(bf16[4,128,2560]{2,1,0:T(8,128)(2,1)} %bitcast.40), calls=%async_computation.1 | async-start | bytes 5242880 | tf_op jit(solution)/shard_map/all_to_all | solution.py:44
  104.4 58.5 %all-to-all-done.1 = bf16[4,128,2560]{2,1,0:T(8,128)(2,1)} async-done(((bf16[4,128,2560]{2,1,0:T(8,128)(2,1)}), bf16[4,128,2560]{2,1,0:T(8,128)(2,1)}, u32[]{:S(2)}, u32[]{:S(2)}) %all-to-all-start.1) | async-done | bytes 2621472 | tf_op jit(solution)/shard_map/all_to_all | solution.py:44
  162.9 3.6 %convert_reduce_fusion = bf16[2,128,2560]{2,1,0:T(8,128)(2,1)} fusion(bf16[4,128,2560]{2,1,0:T(8,128)(2,1)} %all-to-all-done.1), kind=kLoop, calls=%fused_computation.1 | loop fusion | flops 1966080 | bytes 3932160 | tf_op jit(solution)/shard_map/reduce_sum | solution.py:45
  166.5 3.1 %gather_fusion = bf16[128,2560]{1,0:T(8,128)(2,1)S(1)} fusion(bf16[256,2560]{1,0:T(8,128)(2,1)} %bitcast.37, s32[1024]{0:T(1024)S(1)} %pad_clamp_fusion), kind=kCustom, calls=%fused_computation | custom fusion | bytes 1311232 | tf_op jit(solution)/shard_map/jit(_take)/gather | solution.py:46
  169.6 1.0 select_convert_fusion
  170.6 2.2 %copy.7 = bf16[128,2560]{0,1:T(8,128)(2,1)} copy(bf16[128,2560]{1,0:T(8,128)(2,1)} %select_convert_fusion) | data formatting | bytes 1310720
  172.8 20.8 %reduce-scatter.4.cloned.1.call-done = bf16[640,128]{1,0:T(8,128)(2,1)} async-done(((bf16[2560,128]{1,0:T(8,128)(2,1)}), bf16[640,128]{1,0:T(8,128)(2,1)}) %reduce-scatter.4.cloned.1.call-update) | async-done | bytes 163856
  193.6 1.7 copy.8
  (24 shorter events, 0.3 us)
Async XLA Ops:
  6.5 85.9 %copy-start = (bf16[1,512,2560]{2,1,0:T(8,128)(2,1)S(1)}, bf16[1,512,2560]{2,1,0:T(8,128)(2,1)}, u32[]{:S(2)}) copy-start(bf16[1,512,2560]{2,1,0:T(8,128)(2,1)} %param.11) | copy-start | bytes 7864324
  6.5 16.2 %copy-start.2 = (bf16[128,640]{1,0:T(8,128)(2,1)S(1)}, bf16[128,640]{1,0:T(8,128)(2,1)}, u32[]{:S(2)}) copy-start(bf16[128,640]{1,0:T(8,128)(2,1)} %param.6) | copy-start | bytes 491524
  6.5 16.2 %copy-start.3 = (f32[128]{0:T(128)S(1)}, f32[128]{0:T(128)}, u32[]{:S(2)}) copy-start(f32[128]{0:T(128)} %param.7) | copy-start | bytes 1540
  7.7 5.4 %collective-permute-start = (bf16[128,640]{1,0:T(8,128)(2,1)S(1)}, bf16[128,640]{1,0:T(8,128)(2,1)S(1)}, u32[]{:S(2)}, u32[]{:S(2)}) collective-permute-start(bf16[128,640]{1,0:T(8,128)(2,1)S(1)} %multiply_convert_fusion), channel_id=1, source_target_pairs={{0,1},{1,2},{2,3},{3,0},{4,5},{5,6},{6,7},{7,4},{8,9},{9,10},{10,1... | collective-permute-start | bytes 491528 | tf_op jit(solution)/shard_map/ppermute | solution.py:27
  13.1 4.7 %collective-permute-start.1 = (bf16[128,640]{1,0:T(8,128)(2,1)S(1)}, bf16[128,640]{1,0:T(8,128)(2,1)S(1)}, u32[]{:S(2)}, u32[]{:S(2)}) collective-permute-start(bf16[128,640]{1,0:T(8,128)(2,1)S(1)} %collective-permute-done), channel_id=1, source_target_pairs={{0,1},{1,2},{2,3},{3,0},{4,5},{5,6},{6,7},{7,4},{8,9},{9,10},{10,1... | collective-permute-start | bytes 491528 | tf_op jit(solution)/shard_map/ppermute | solution.py:27
  17.9 4.7 %collective-permute-start.2 = (bf16[128,640]{1,0:T(8,128)(2,1)S(1)}, bf16[128,640]{1,0:T(8,128)(2,1)S(1)}, u32[]{:S(2)}, u32[]{:S(2)}) collective-permute-start(bf16[128,640]{1,0:T(8,128)(2,1)S(1)} %collective-permute-done.1), channel_id=1, source_target_pairs={{0,1},{1,2},{2,3},{3,0},{4,5},{5,6},{6,7},{7,4},{8,9},{9,10},{10,1... | collective-permute-start | bytes 491528 | tf_op jit(solution)/shard_map/ppermute | solution.py:27
  23.9 66.0 %copy-start.5 = (bf16[1,2560,512]{2,1,0:T(8,128)(2,1)S(1)}, bf16[1,2560,512]{2,1,0:T(8,128)(2,1)}, u32[]{:S(2)}) copy-start(bf16[1,2560,512]{2,1,0:T(8,128)(2,1)} %param.9) | copy-start | bytes 7864324
  88.4 1.5 copy-start.1
  99.6 4.7 %copy-start.4 = (s32[128,1]{0,1:T(1,128)S(1)}, s32[128,1]{0,1:T(1,128)}, u32[]{:S(2)}) copy-start(s32[128,1]{0,1:T(1,128)} %param.8) | copy-start | bytes 1540
  99.6 63.2 %all-to-all-start.1 = ((bf16[4,128,2560]{2,1,0:T(8,128)(2,1)}), bf16[4,128,2560]{2,1,0:T(8,128)(2,1)}, u32[]{:S(2)}, u32[]{:S(2)}) async-start(bf16[4,128,2560]{2,1,0:T(8,128)(2,1)} %bitcast.40), calls=%async_computation.1 | async-start | bytes 5242880 | tf_op jit(solution)/shard_map/all_to_all | solution.py:44
  104.3 89.3 %reduce-scatter.4.cloned.1.call-start = ((), (), s32[]{:S(2)}) async-start(), calls=%async_computation.3 | async-start | bytes 819200
Sparse Core Ops, SparseCore 0:
  172.9 20.6 reduce-scatter.3
